TPU v7x, 512 devices: a whole 4x4x16 slice. The times are simulated.
512 devices in a mesh: wa: 32 (over x, y, core), ha: 16 (over z).
Axes of the slice: x: 4, y: 4, z: 16, core: 2. Of those that a mesh axis runs over, the one named last changes fastest.
Arguments:
- residual_in: bfloat16 [192, 16384], P('ha', 'wa'), may hold values from -43.25 to 43.25
- grad_out: bfloat16 [192, 16384], P('ha', 'wa'), may hold values from -6 to 6
- norm_gain: bfloat16 [16384], P('wa'), may hold values from 0.099609375 to 1.8984375
- w_gate: bfloat16 [16384, 26624], P('wa', 'ha'), may hold values from -0.0390625 to 0.0390625
- w_up: bfloat16 [16384, 26624], P('wa', 'ha'), may hold values from -0.0390625 to 0.0390625
- w_down: bfloat16 [26624, 16384], P('ha', 'wa'), may hold values from -0.030643146 to 0.030643146
Outputs:
- grad_in: bfloat16 [192, 16384], P('ha', 'wa')
All inputs are finite; a program needn't handle non-finite values.
Results may differ from a plain program's by a relative error of at most 0.0053.
Values may be sent and summed in bfloat16 or wider, within the bound.
No kernel may reach another device: no remote copies, remote signals or barrier semaphores. Data moves between devices by JAX's collectives and lax.ppermute only.
A program may use at most 64 MiB of HBM per device.

v0:
```python
import jax
import jax.numpy as jnp
from jax import lax
from jax.sharding import Mesh
from jax.sharding import PartitionSpec as P

D = 16384
WA = ("x", "y", "core")


def gate_grads(gate, up, d_hidden):
    sig = jax.nn.sigmoid(gate)
    d_up = (d_hidden * gate * sig).astype(jnp.bfloat16)
    d_gate = (d_hidden * up * sig * (1.0 + gate * (1.0 - sig))).astype(jnp.bfloat16)
    return (d_gate, d_up)


def local(residual_in, grad_out, norm_gain, w_gate, w_up, w_down):
    rows = residual_in.shape[0]
    gain_f = norm_gain.astype(jnp.float32)
    piece = lax.all_gather(jnp.stack([residual_in, grad_out]), "ha", axis=1, tiled=True)
    stream_all = piece[0].astype(jnp.float32)
    squares = jnp.sum(stream_all * stream_all, axis=1)
    squares = lax.psum(lax.psum(lax.psum(squares, "core"), "y"), "x")
    inv_rms_all = lax.rsqrt(squares / D + 1e-05)[:, None]
    normed = (stream_all * inv_rms_all * gain_f).astype(jnp.bfloat16)
    gate_part = jnp.dot(normed, w_gate, preferred_element_type=jnp.float32)
    up_part = jnp.dot(normed, w_up, preferred_element_type=jnp.float32)
    back_part = lax.dot_general(
        piece[1], w_down, (((1,), (1,)), ((), ())), preferred_element_type=jnp.float32
    )
    summed = lax.psum(jnp.stack([gate_part, up_part, back_part]), WA)
    gate, up, d_hidden = (summed[0], summed[1], summed[2])
    d_gate, d_up = gate_grads(gate, up, d_hidden)
    dot_part = jnp.sum(d_gate.astype(jnp.float32) * gate + d_up.astype(jnp.float32) * up, axis=1)
    total = lax.dot_general(
        d_gate, w_gate, (((1,), (1,)), ((), ())), preferred_element_type=jnp.float32
    ) + lax.dot_general(d_up, w_up, (((1,), (1,)), ((), ())), preferred_element_type=jnp.float32)
    n_ha, width = (lax.axis_size("ha"), total.shape[1])
    dot_rows = jnp.pad(dot_part.reshape(n_ha, 1, rows), ((0, 0), (0, 0), (0, width - rows)))
    packed = jnp.concatenate([total.reshape(n_ha, rows, width), dot_rows], axis=1)
    mine = lax.psum_scatter(packed.reshape(-1, width), "ha", scatter_dimension=0, tiled=True)
    d_normed = mine[:rows]
    start = lax.axis_index("ha") * rows
    inv_rms = lax.dynamic_slice_in_dim(inv_rms_all, start, rows, axis=0)
    row_dot = mine[rows, :rows][:, None] / inv_rms
    stream = residual_in.astype(jnp.float32)
    scaled = d_normed * gain_f
    grad_in = grad_out.astype(jnp.float32) + inv_rms * scaled - stream * inv_rms**3 * row_dot / D
    return grad_in.astype(jnp.bfloat16)


def solution(mesh):
    devices = mesh.devices if mesh.axis_names[0] == "wa" else mesh.devices.T
    view = Mesh(devices.reshape(4, 4, 2, devices.shape[1]), WA + ("ha",))
    placed = (P("ha", WA), P("ha", WA), P(WA), P(WA, "ha"), P(WA, "ha"), P("ha", WA))
    return jax.shard_map(local, mesh=view, in_specs=placed, out_specs=P("ha", WA), check_vma=False)
```

profile of v0, /device:TPU:2, one launch (start us, length us, event | category | flops | bytes accessed | tf_op | source)
XLA Modules:
  0.0 363.5 jit_solution(15139991436451758172)
XLA Ops:
  6.5 0.0 copy-start
  6.5 0.0 copy-start.8
  6.5 0.0 copy-start.1
  6.5 0.0 all-reduce.5.cloned.1.call-start
  6.5 0.9 pad_maximum_fusion.1
  7.5 37.8 %all_gather.3 = bf16[2,192,512]{2,0,1:T(2,128)(2,1)S(1)} all-gather(bf16[2,12,512]{2,0,1:T(2,128)(2,1)S(1)} %copy.9), channel_id=1, replica_groups=mesh['x'=4,'y'=4,'core'=2,'ha'=16] {'ha'}, dimensions={1}, use_global_device_ids=true | all-gather | bytes 417792 | tf_op jit(solution)/shard_map/all_gather | solution.py:21
  45.3 1.3 slice_convert_fusion
  46.6 0.0 copy-start.2
  46.6 0.7 copy-done.2
  47.3 0.1 fusion
  47.4 2.5 psum.28
  49.9 10.7 %psum.29 = f32[192]{0:T(256)S(1)} all-reduce(f32[192]{0:T(256)S(1)} %psum.28), channel_id=1, replica_groups=mesh['x'=4,'y'=4,'core'=2,'ha'=16] {'y'}, use_global_device_ids=true, to_apply=%region_2.0 | all-reduce | flops 192 | bytes 1536 | tf_op jit(solution)/shard_map/psum | solution.py:24
  60.6 8.6 %psum.30 = f32[192]{0:T(256)S(1)} all-reduce(f32[192]{0:T(256)S(1)} %psum.29), channel_id=1, replica_groups=mesh['x'=4,'y'=4,'core'=2,'ha'=16] {'x'}, use_global_device_ids=true, to_apply=%region_3.0 | all-reduce | flops 192 | bytes 1536 | tf_op jit(solution)/shard_map/psum | solution.py:24
  69.2 0.0 copy-done.8
  69.2 0.0 copy-done.1
  69.2 0.0 copy-start.3
  69.3 1.6 convolution_bitcast_fusion.1
  70.9 0.0 copy-done
  70.9 0.0 copy-done.3
  70.9 0.0 copy-start.4
  70.9 0.0 copy-start.5
  70.9 0.6 convolution_bitcast_fusion.2
  71.5 0.8 copy-done.4
  72.4 0.1 copy-done.5
  72.4 0.7 convolution_bitcast_fusion
  73.2 2.1 pad_maximum_fusion
  75.3 0.0 all-reduce.5.cloned.1.call-update
  75.3 0.0 all-reduce.7.cloned.1.call-start
  75.4 134.0 %all-reduce.5.cloned.1.call-done = f32[3,192,1664]{2,1,0:T(8,128)} async-done(((f32[3,192,1664]{2,1,0:T(8,128)}), f32[3,192,1664]{2,1,0:T(8,128)}) %all-reduce.5.cloned.1.call-update) | async-done | bytes 3833872 | tf_op jit(solution)/shard_map/psum | solution.py:32
  209.3 2.9 add_reduce_fusion
  212.3 0.7 fusion.11
  213.0 1.5 convolution_add_fusion
  214.5 1.0 reshape.21
  215.5 0.0 copy-start.6
  215.5 0.0 copy-start.7
  215.5 0.1 reshape.22
  215.6 0.1 select_maximum_fusion
  215.7 0.8 reshape.23
  216.5 0.0 all-reduce.7.cloned.1.call-update
  216.5 1.3 dynamic-slice.4
  218.4 0.1 multiply_multiply_fusion
  218.5 136.0 %all-reduce.7.cloned.1.call-done = f32[208,512]{1,0:T(8,128)} async-done(((f32[208,512]{1,0:T(8,128)}), f32[208,512]{1,0:T(8,128)}) %all-reduce.7.cloned.1.call-update) | async-done | bytes 426000
  354.5 0.7 fusion.8
  355.2 0.0 copy-done.6
  355.2 0.0 copy-done.7
  355.2 1.5 fusion.6
  (3 shorter events, 0.0 us)
Async XLA Ops:
  6.5 64.4 %copy-start = (bf16[512,1664]{1,0:T(8,128)(2,1)S(1)}, bf16[512,1664]{1,0:T(8,128)(2,1)}, u32[]{:S(2)}) copy-start(bf16[512,1664]{1,0:T(8,128)(2,1)} %param.9) | copy-start | bytes 5111812
  6.5 62.7 %copy-start.8 = (bf16[512]{0:T(512)(128)(2,1)S(1)}, bf16[512]{0:T(512)(128)(2,1)}, u32[]{:S(2)}) copy-start(bf16[512]{0:T(512)(128)(2,1)} %param.8) | copy-start | bytes 3076
  6.5 62.7 %copy-start.1 = (bf16[512,1664]{1,0:T(8,128)(2,1)S(1)}, bf16[512,1664]{1,0:T(8,128)(2,1)}, u32[]{:S(2)}) copy-start(bf16[512,1664]{1,0:T(8,128)(2,1)} %param.10) | copy-start | bytes 5111812
  6.5 202.8 %all-reduce.5.cloned.1.call-start = ((), (), s32[]{:S(2)}) async-start(), calls=%async_computation | async-start | bytes 7667712 | tf_op jit(solution)/shard_map/psum | solution.py:32
  46.6 0.7 copy-start.2
  69.2 1.7 copy-start.3
  70.9 1.5 copy-start.4
  70.9 1.5 copy-start.5
  75.3 279.2 %all-reduce.7.cloned.1.call-start = ((), (), s32[]{:S(2)}) async-start(), calls=%async_computation.1 | async-start | bytes 851968
  215.5 139.7 %copy-start.6 = (bf16[12,512]{1,0:T(8,128)(2,1)S(1)}, bf16[12,512]{1,0:T(8,128)(2,1)}, u32[]{:S(2)}) copy-start(bf16[12,512]{1,0:T(8,128)(2,1)} %param.7) | copy-start | bytes 36868
  215.5 139.7 %copy-start.7 = (bf16[12,512]{1,0:T(8,128)(2,1)S(1)}, bf16[12,512]{1,0:T(8,128)(2,1)}, u32[]{:S(2)}) copy-start(bf16[12,512]{1,0:T(8,128)(2,1)} %param.6) | copy-start | bytes 36868
Sparse Core Ops, SparseCore 0:
  75.4 133.8 all-reduce.4
  216.6 137.8 all-reduce.6
where the time goes:
time: 364 us
  waiting for transfers between devices  270 us (74%)
  blocking collectives  59.6 us (16%)
  between operations  14.2 us (4%)
  other arithmetic  9.68 us (3%)
  matrix products  5.11 us (1%)
  local copies, waits for them, and re-layouts  4.91 us (1%)
    unnamed x3, waiting for transfers between devices  136 us
    psum x1, waiting for transfers between devices, local(): summed = lax.psum(jnp.stack([gate_part, up_part, back_part]), WA)  134 us
    all_gather x1, blocking collectives, local(): lax.all_gather(jnp.stack([residual_in, grad_out]), 'ha', axis=1, tiled=True)  37.8 us
    psum x3, blocking collectives, local(): squares = lax.psum(lax.psum(lax.psum(squares, 'core'), 'y'), 'x')  21.8 us
  transfers between devices with their start and end apart: 2, of which 2 were waited for; matrix products, arithmetic and copies ran while one was open for 0% of the time, Pallas kernels for 0%

commit v1 on v0

--- a/solution.py
+++ b/solution.py
@@ -18,7 +18,12 @@
 def local(residual_in, grad_out, norm_gain, w_gate, w_up, w_down):
     rows = residual_in.shape[0]
     gain_f = norm_gain.astype(jnp.float32)
-    piece = lax.all_gather(jnp.stack([residual_in, grad_out]), "ha", axis=1, tiled=True)
+    piece = jnp.concatenate(
+        lax.all_to_all(
+            jnp.stack([jnp.stack([residual_in, grad_out])] * lax.axis_size("ha")), "ha", 0, 0
+        ),
+        axis=1,
+    )
     stream_all = piece[0].astype(jnp.float32)
     squares = jnp.sum(stream_all * stream_all, axis=1)
     squares = lax.psum(lax.psum(lax.psum(squares, "core"), "y"), "x")

time: 364 us -> 376 us (1.033)
  blocking collectives: 59.6 us -> 21.8 us
  waiting for transfers between devices: 270 us -> 293 us
  starting transfers between devices: 0.04 us -> 15.3 us
  local copies, waits for them, and re-layouts: 4.91 us -> 10.7 us
  matrix products: 5.11 us -> 8.93 us
    all_gather x1 -> x0, blocking collectives: 37.8 us -> none  [local(): lax.all_gather(jnp.stack([residual_in, grad_out]), 'ha', axis=1, tiled=True)]
    all_to_all x0 -> x1, waiting for transfers between devices: none -> 23.8 us  [local(): lax.all_to_all(jnp.stack([jnp.stack([residual_in, grad_out])] * lax.axis_...]
    all_to_all x0 -> x1, starting transfers between devices: none -> 15.2 us  [local(): lax.all_to_all(jnp.stack([jnp.stack([residual_in, grad_out])] * lax.axis_...]
  transfers between devices with their start and end apart: 2 -> 3, of which waited for: 2 -> 3; matrix products, arithmetic and copies ran while one was open for 0% -> 0% of each run, Pallas kernels for 0% -> 0%
where the time goes in v1:
time: 376 us
  waiting for transfers between devices  293 us (78%)
  blocking collectives  21.8 us (6%)
  starting transfers between devices  15.3 us (4%)
  between operations  14.2 us (4%)
  other arithmetic  11.7 us (3%)
  local copies, waits for them, and re-layouts  10.7 us (3%)
  matrix products  8.93 us (2%)
    unnamed x3, waiting for transfers between devices  136 us
    psum x1, waiting for transfers between devices, local(): summed = lax.psum(jnp.stack([gate_part, up_part, back_part]), WA)  133 us
    all_to_all x1, waiting for transfers between devices, local(): lax.all_to_all(jnp.stack([jnp.stack([residual_in, grad_out])] * lax.axis_...  23.8 us
    psum x3, blocking collectives, local(): squares = lax.psum(lax.psum(lax.psum(squares, 'core'), 'y'), 'x')  21.8 us
    all_to_all x1, starting transfers between devices, local(): lax.all_to_all(jnp.stack([jnp.stack([residual_in, grad_out])] * lax.axis_...  15.2 us
  transfers between devices with their start and end apart: 3, of which 3 were waited for; matrix products, arithmetic and copies ran while one was open for 0% of the time, Pallas kernels for 0%

profile of v1, /device:TPU:2, one launch (start us, length us, event | category | flops | bytes accessed | tf_op | source)
XLA Modules:
  0.0 375.6 jit_solution(295224722900182479)
XLA Ops:
  6.5 0.0 copy-start
  6.5 0.0 copy-start.7
  6.5 0.9 pad_maximum_fusion.1
  7.5 0.9 stack.19
  8.4 15.2 %all-to-all-start = ((bf16[16,2,12,512]{3,1,2,0:T(2,128)(2,1)}), bf16[16,2,12,512]{3,1,2,0:T(2,128)(2,1)}, u32[]{:S(2)}, u32[]{:S(2)}) async-start(bf16[16,2,12,512]{3,1,2,0:T(2,128)(2,1)} %stack.19), calls=%async_computation | async-start | bytes 786432 | tf_op jit(solution)/shard_map/all_to_all | solution.py:22
  23.6 0.0 copy-start.1
  23.7 0.0 all-reduce.5.cloned.1.call-start
  23.7 0.0 copy-done.7
  23.7 23.8 %all-to-all-done = bf16[16,2,12,512]{3,1,2,0:T(2,128)(2,1)} async-done(((bf16[16,2,12,512]{3,1,2,0:T(2,128)(2,1)}), bf16[16,2,12,512]{3,1,2,0:T(2,128)(2,1)}, u32[]{:S(2)}, u32[]{:S(2)}) %all-to-all-start) | async-done | bytes 393248 | tf_op jit(solution)/shard_map/all_to_all | solution.py:22
  47.5 3.4 multiply_reduce_fusion
  50.9 2.9 slice_reduce_fusion
  53.8 0.1 reduce_sum.21
  53.9 2.5 psum.28
  56.3 10.7 %psum.29 = f32[192]{0:T(256)S(1)} all-reduce(f32[192]{0:T(256)S(1)} %psum.28), channel_id=1, replica_groups=mesh['x'=4,'y'=4,'core'=2,'ha'=16] {'y'}, use_global_device_ids=true, to_apply=%region_2.0 | all-reduce | flops 192 | bytes 1536 | tf_op jit(solution)/shard_map/psum | solution.py:29
  67.0 8.6 %psum.30 = f32[192]{0:T(256)S(1)} all-reduce(f32[192]{0:T(256)S(1)} %psum.29), channel_id=1, replica_groups=mesh['x'=4,'y'=4,'core'=2,'ha'=16] {'x'}, use_global_device_ids=true, to_apply=%region_3.0 | all-reduce | flops 192 | bytes 1536 | tf_op jit(solution)/shard_map/psum | solution.py:29
  75.7 1.8 reshape.36
  77.5 0.0 copy-done.1
  77.5 0.0 copy-start.4
  77.5 2.7 convolution_bitcast_fusion.1
  80.2 0.0 copy-done
  80.2 0.0 copy-done.4
  80.2 1.6 convolution_bitcast_fusion.2
  81.9 1.7 squeeze.13
  83.5 0.0 copy-start.2
  83.5 0.0 copy-start.3
  83.5 2.4 convolution_bitcast_fusion
  85.9 0.0 copy-done.2
  86.0 0.0 copy-done.3
  86.0 2.1 pad_maximum_fusion
  88.1 0.0 all-reduce.5.cloned.1.call-update
  88.1 0.0 all-reduce.7.cloned.1.call-start
  88.2 133.3 %all-reduce.5.cloned.1.call-done = f32[3,192,1664]{2,1,0:T(8,128)} async-done(((f32[3,192,1664]{2,1,0:T(8,128)}), f32[3,192,1664]{2,1,0:T(8,128)}) %all-reduce.5.cloned.1.call-update) | async-done | bytes 3833872 | tf_op jit(solution)/shard_map/psum | solution.py:37
  221.5 2.9 add_reduce_fusion
  224.4 0.7 fusion.7
  225.1 1.5 convolution_add_fusion
  226.6 1.0 reshape.33
  227.6 0.0 copy-start.5
  227.6 0.0 copy-start.6
  227.6 0.1 reshape.34
  227.7 0.1 select_maximum_fusion
  227.8 0.8 reshape.35
  228.6 0.0 all-reduce.7.cloned.1.call-update
  228.6 1.3 dynamic-slice.4
  230.6 0.1 multiply_multiply_fusion
  230.6 136.0 %all-reduce.7.cloned.1.call-done = f32[208,512]{1,0:T(8,128)} async-done(((f32[208,512]{1,0:T(8,128)}), f32[208,512]{1,0:T(8,128)}) %all-reduce.7.cloned.1.call-update) | async-done | bytes 426000
  366.6 0.7 fusion.6
  367.3 0.0 copy-done.5
  367.3 0.0 copy-done.6
  367.3 1.5 fusion.4
  (3 shorter events, 0.0 us)
Async XLA Ops:
  6.5 73.7 %copy-start = (bf16[512,1664]{1,0:T(8,128)(2,1)S(1)}, bf16[512,1664]{1,0:T(8,128)(2,1)}, u32[]{:S(2)}) copy-start(bf16[512,1664]{1,0:T(8,128)(2,1)} %param.9) | copy-start | bytes 5111812
  6.5 17.2 %copy-start.7 = (bf16[512]{0:T(512)(128)(2,1)S(1)}, bf16[512]{0:T(512)(128)(2,1)}, u32[]{:S(2)}) copy-start(bf16[512]{0:T(512)(128)(2,1)} %param.8) | copy-start | bytes 3076
  8.4 39.1 %all-to-all-start = ((bf16[16,2,12,512]{3,1,2,0:T(2,128)(2,1)}), bf16[16,2,12,512]{3,1,2,0:T(2,128)(2,1)}, u32[]{:S(2)}, u32[]{:S(2)}) async-start(bf16[16,2,12,512]{3,1,2,0:T(2,128)(2,1)} %stack.19), calls=%async_computation | async-start | bytes 786432 | tf_op jit(solution)/shard_map/all_to_all | solution.py:22
  23.6 53.9 %copy-start.1 = (bf16[512,1664]{1,0:T(8,128)(2,1)S(1)}, bf16[512,1664]{1,0:T(8,128)(2,1)}, u32[]{:S(2)}) copy-start(bf16[512,1664]{1,0:T(8,128)(2,1)} %param.10) | copy-start | bytes 5111812
  23.7 197.8 %all-reduce.5.cloned.1.call-start = ((), (), s32[]{:S(2)}) async-start(), calls=%async_computation.1 | async-start | bytes 7667712 | tf_op jit(solution)/shard_map/psum | solution.py:37
  77.5 2.7 copy-start.4
  83.5 2.4 copy-start.2
  83.5 2.4 copy-start.3
  88.1 278.5 %all-reduce.7.cloned.1.call-start = ((), (), s32[]{:S(2)}) async-start(), calls=%async_computation.2 | async-start | bytes 851968
  227.6 139.7 %copy-start.5 = (bf16[12,512]{1,0:T(8,128)(2,1)S(1)}, bf16[12,512]{1,0:T(8,128)(2,1)}, u32[]{:S(2)}) copy-start(bf16[12,512]{1,0:T(8,128)(2,1)} %param.7) | copy-start | bytes 36868
  227.6 139.7 %copy-start.6 = (bf16[12,512]{1,0:T(8,128)(2,1)S(1)}, bf16[12,512]{1,0:T(8,128)(2,1)}, u32[]{:S(2)}) copy-start(bf16[12,512]{1,0:T(8,128)(2,1)} %param.6) | copy-start | bytes 36868
Sparse Core Ops, SparseCore 0:
  88.2 133.1 all-reduce.4
  228.7 137.8 all-reduce.6
